TPU v7x, 32 devices: a whole 2x2x4 slice. The times are simulated.
32 devices in a mesh: cuts: 2 (over x), mode: 16 (over z, y, core).
Axes of the slice: x: 2, y: 2, z: 4, core: 2. Of those that a mesh axis runs over, the one named last changes fastest.
Arguments:
- stem_blocks: bfloat16 [2, 4096, 2, 256], P('cuts', 'mode'), may hold values from -6 to 6
- w1_table: bfloat16 [8, 2, 256, 256], replicated, may hold values from -0.25 to 0.25
- w2_table: bfloat16 [8, 2, 256, 256], replicated, may hold values from -0.125 to 0.125
- slice_ids: int32 [2, 2, 2], P('cuts'), may hold values from 0 to 7, as said below
- mode_perm: int32 [256], replicated, may hold values from 0 to 255, each once
Outputs:
- amplitudes: float32 [256, 16, 2, 256], P('mode', 'cuts')
Inputs may be any that keep to these rules, and one draw needn't show every extreme that they name: For each stem block b, the 2 values slice_ids[:,b,0] are distinct, and so are the 2 values slice_ids[:,b,1]. `mode_perm`: each column appears once.
All inputs are finite; a program needn't handle non-finite values.
Results may differ from a plain program's by a relative error of at most 0.0029.
Values may be sent and summed in bfloat16 or wider, within the bound.
No kernel may reach another device: no remote copies, remote signals or barrier semaphores. Data moves between devices by JAX's collectives and lax.ppermute only.
A program may use at most 64 MiB of HBM per device.

v0:
```python
import jax
import jax.numpy as jnp
from jax import lax
from jax.sharding import PartitionSpec as P


def broadcast(block, axis, source):
    block = jnp.where(lax.axis_index(axis) == source, block, jnp.zeros_like(block))
    return lax.psum(block, axis)


def widen_first(entry):
    real_part, imag_part = (entry[0], entry[1])
    upper = jnp.concatenate([real_part, imag_part], axis=1)
    lower = jnp.concatenate([-imag_part, real_part], axis=1)
    return jnp.concatenate([upper, lower], axis=0)


def widen_second(entry):
    real_part, imag_part = (entry[0], entry[1])
    first_row = jnp.concatenate([real_part, imag_part], axis=1)
    second_row = jnp.concatenate([-imag_part, real_part], axis=1)
    return jnp.stack([first_row, second_row], axis=0)


def second_step(exchanged, weight_two, contract_cols, free_cols):
    block_count, mode_count, piece_rows, _ = exchanged.shape
    pieces = exchanged.reshape(block_count, mode_count, piece_rows, 2, contract_cols, free_cols)
    wide_out = weight_two.shape[3]
    shaped = weight_two.reshape(block_count, 2, mode_count, contract_cols, wide_out)
    return jnp.einsum("nhqpcs,nphco->qso", pieces, shaped, preferred_element_type=jnp.float32)


def on_device(stem_blocks, w1_table, w2_table, slice_ids, mode_perm):
    mode_count = lax.axis_size("mode")
    row_count = stem_blocks.shape[1]
    stem_width = stem_blocks.shape[3]
    mid_width = w1_table.shape[3]
    inner_width = w2_table.shape[2]
    out_width = w2_table.shape[3]
    piece_rows = row_count // mode_count
    contract_cols = inner_width // mode_count
    free_cols = mid_width // contract_cols
    block_count = slice_ids.shape[1]
    first_all = jax.vmap(widen_first)(jnp.take(w1_table, mode_perm, axis=3))
    second_all = jax.vmap(widen_second)(w2_table)
    own_slices = slice_ids[0]
    begin = jnp.zeros((piece_rows, free_cols, 2 * out_width), jnp.float32)

    def one_block(block_index, running):
        stem_part = broadcast(stem_blocks[0], "cuts", block_index)
        slice_pair = own_slices[block_index]
        weight_one = lax.dynamic_index_in_dim(first_all, slice_pair[0], 0, keepdims=False)
        product = jnp.dot(
            stem_part.reshape(row_count, 2 * stem_width),
            weight_one,
            preferred_element_type=jnp.float32,
        ).astype(jnp.bfloat16)
        exchanged = lax.all_to_all(
            product[None, None], "mode", split_axis=2, concat_axis=1, tiled=True
        )
        weight_two = lax.dynamic_index_in_dim(second_all, slice_pair[1], 0, keepdims=True)
        return running + second_step(exchanged, weight_two, contract_cols, free_cols)

    amplitude = lax.fori_loop(0, block_count, one_block, begin)
    summed = lax.psum_scatter(amplitude, "cuts", scatter_dimension=1, tiled=True)
    return summed.reshape(piece_rows, summed.shape[1], 2, out_width)


def solution(mesh):
    placed = (P("cuts", "mode", None, None), P(), P(), P("cuts", None, None), P())
    return jax.shard_map(
        on_device,
        mesh=mesh,
        in_specs=placed,
        out_specs=P("mode", "cuts", None, None),
        check_vma=False,
    )
```

profile of v0, /device:TPU:0, one launch (start us, length us, event | category | flops | bytes accessed | tf_op | source)
XLA Modules:
  0.0 173.1 jit_solution(13787529332660151836)
XLA Ops:
  7.4 3.2 %slice_bitcast_fusion.2 = (bf16[8,256,256]{2,1,0:T(8,128)(2,1)}, bf16[8,256,256]{2,1,0:T(8,128)(2,1)}) fusion(bf16[8,2,256,256]{3,2,1,0:T(8,128)(2,1)} %param.9), kind=kLoop, calls=%fused_computation.19 | loop fusion | bytes 4194304 | tf_op jit(solution)/shard_map/vmap()/squeeze | solution.py:20
  10.6 1.1 fusion.6
  11.7 0.9 copy-done.6
  12.6 3.1 %copy.29 = bf16[8,2,256,256]{2,0,3,1:T(8,128)(2,1)} copy(bf16[8,2,256,256]{3,2,1,0:T(8,128)(2,1)S(1)} %copy-done.6) | data formatting | bytes 4194304 | tf_op args[1]
  15.7 2.4 %gather_fusion = bf16[256,8,2,256]{3,1,2,0:T(8,128)(2,1)S(1)} fusion(bf16[8,2,256,256]{2,0,3,1:T(8,128)(2,1)} %copy.29, s32[1024]{0:T(1024)S(1)} %pad_clamp_fusion), kind=kCustom, calls=%fused_computation | custom fusion | bytes 4195328 | tf_op jit(solution)/shard_map/jit(_take)/gather | solution.py:45
  18.1 0.9 select_bitcast_fusion
  19.0 1.1 slice_bitcast_fusion
  20.2 13.0 %maximum_maximum_fusion = bf16[8,512,512]{1,0,2:T(8,128)(2,1)} fusion(bf16[8,256,256]{1,0,2:T(8,128)(2,1)} %get-tuple-element.171, bf16[8,256,256]{1,0,2:T(8,128)(2,1)S(1)} %fusion.7, bf16[8,256,256]{1,0,2:T(8,128)(2,1)S(1)} %get-tuple-element.170), kind=kLoop, calls=%fused_computation.12 | loop fusion | flops 16777216 | bytes 7340032 | tf_op jit(solution)/shard_map/vmap()/concatenate | solution.py:16
  33.3 7.7 %copy.34 = bf16[8,512,512]{2,1,0:T(8,128)(2,1)} copy(bf16[8,512,512]{1,0,2:T(8,128)(2,1)} %maximum_maximum_fusion) | data formatting | bytes 8388608
  41.0 1.9 %maximum_bitcast_fusion.1 = (bf16[1,8,256,512]{3,2,0,1:T(8,128)(2,1)S(1)}, bf16[1,8,256,512]{3,2,0,1:T(8,128)(2,1)S(1)}) fusion(bf16[8,256,256]{2,1,0:T(8,128)(2,1)S(1)} %copy-done.5, bf16[8,256,256]{2,1,0:T(8,128)(2,1)} %get-tuple-element.169, bf16[8,256,256]{2,1,0:T(8,128)(2,1)S(1)} %copy-done.4), kind=kLoop, calls=%fused_computation.14 | loop fusion | flops 8388608 | bytes 7340032 | tf_op jit(solution)/shard_map/vmap()/stack | solution.py:23
  42.9 2.3 %maximum_bitcast_fusion = bf16[8,2,256,512]{3,2,1,0:T(8,128)(2,1)} fusion(bf16[1,8,256,512]{3,2,0,1:T(8,128)(2,1)S(1)} %get-tuple-element.173, bf16[1,8,256,512]{3,2,0,1:T(8,128)(2,1)S(1)} %get-tuple-element.172), kind=kLoop, calls=%fused_computation.13 | loop fusion | flops 2097152 | bytes 8388608 | tf_op jit(solution)/shard_map/vmap()/transpose | solution.py:46
  45.3 104.0 %while.14 = (s32[]{:T(128)}, f32[16,16,512]{2,1,0:T(8,128)S(1)}, bf16[1,256,2,256]{3,2,1,0:T(2,128)(2,1)S(1)}, s32[2,2]{1,0:T(2,128)S(1)}, bf16[8,512,512]{2,1,0...) while((s32[]{:T(128)}, f32[16,16,512]{2,1,0:T(8,128)S(1)}, ...), condition=%wide.region_2.3_spmd.clone, body=%wide.region_0.0_spmd.clone.sunk | while | flops 269090816 | bytes 11534731 | solution.py:65
  48.9 25.5 %all-reduce.2.cloned.1.call-done = bf16[256,512]{1,0:T(8,128)(2,1)} async-done(((bf16[256,512]{1,0:T(8,128)(2,1)}), bf16[256,512]{1,0:T(8,128)(2,1)}) %all-reduce.2.cloned.1.call-update) | async-done | bytes 262160 | tf_op jit(solution)/shard_map/while/body/eval_jaxpr/psum | solution.py:9
  74.4 1.4 fusion.23
  76.7 2.2 %reduce.6 = bf16[256,512]{1,0:T(8,128)(2,1)S(1)} reduce(bf16[256,1,1,512]{3,2,1,0:T(2,128)(2,1)S(1)} %bitcast.79, bf16[]{:T(256)} %broadcast.40), dimensions={1,2}, to_apply=%bitcast.54.reduce_sub_computation | reduce | bytes 524290 | tf_op jit(solution)/shard_map/while
  79.0 0.9 reshape.66
  79.8 5.6 %all-to-all-start = ((bf16[16,2,4096]{2,1,0:T(2,128)(2,1)}), bf16[16,2,4096]{2,1,0:T(2,128)(2,1)S(1)}, u32[]{:S(2)}, u32[]{:S(2)}) async-start(bf16[16,2,4096]{2,1,0:T(2,128)(2,1)} %reshape.66), calls=%async_computation | async-start | bytes 524288 | tf_op jit(solution)/shard_map/while/body/eval_jaxpr/all_to_all | solution.py:59
  87.5 1.1 constant_dynamic-slice_fusion.5
  88.6 6.9 %all-to-all-done = bf16[16,2,4096]{2,1,0:T(2,128)(2,1)S(1)} async-done(((bf16[16,2,4096]{2,1,0:T(2,128)(2,1)}), bf16[16,2,4096]{2,1,0:T(2,128)(2,1)S(1)}, u32[]{:S(2)}, u32[]{:S(2)}) %all-to-all-start) | async-done | bytes 262176 | tf_op jit(solution)/shard_map/while/body/eval_jaxpr/all_to_all | solution.py:59
  95.8 1.5 bitcast_reduce_fusion.2
  97.3 1.7 reshape.68
  103.5 20.2 %all-reduce.2.cloned.1.call-done = bf16[256,512]{1,0:T(8,128)(2,1)} async-done(((bf16[256,512]{1,0:T(8,128)(2,1)}), bf16[256,512]{1,0:T(8,128)(2,1)}) %all-reduce.2.cloned.1.call-update) | async-done | bytes 262160 | tf_op jit(solution)/shard_map/while/body/eval_jaxpr/psum | solution.py:9
  123.7 1.4 fusion.23
  126.1 2.2 %reduce.6 = bf16[256,512]{1,0:T(8,128)(2,1)S(1)} reduce(bf16[256,1,1,512]{3,2,1,0:T(2,128)(2,1)S(1)} %bitcast.79, bf16[]{:T(256)} %broadcast.40), dimensions={1,2}, to_apply=%bitcast.54.reduce_sub_computation | reduce | bytes 524290 | tf_op jit(solution)/shard_map/while
  128.3 0.9 reshape.66
  129.2 5.6 %all-to-all-start = ((bf16[16,2,4096]{2,1,0:T(2,128)(2,1)}), bf16[16,2,4096]{2,1,0:T(2,128)(2,1)S(1)}, u32[]{:S(2)}, u32[]{:S(2)}) async-start(bf16[16,2,4096]{2,1,0:T(2,128)(2,1)} %reshape.66), calls=%async_computation | async-start | bytes 524288 | tf_op jit(solution)/shard_map/while/body/eval_jaxpr/all_to_all | solution.py:59
  136.9 1.1 constant_dynamic-slice_fusion.5
  138.0 6.9 %all-to-all-done = bf16[16,2,4096]{2,1,0:T(2,128)(2,1)S(1)} async-done(((bf16[16,2,4096]{2,1,0:T(2,128)(2,1)}), bf16[16,2,4096]{2,1,0:T(2,128)(2,1)S(1)}, u32[]{:S(2)}, u32[]{:S(2)}) %all-to-all-start) | async-done | bytes 262176 | tf_op jit(solution)/shard_map/while/body/eval_jaxpr/all_to_all | solution.py:59
  145.1 1.5 bitcast_reduce_fusion.2
  146.6 1.7 reshape.68
  150.1 13.7 %reduce-scatter.2.cloned.1.call-done = f32[16,8,512]{2,1,0:T(8,128)} async-done(((f32[16,16,512]{2,1,0:T(8,128)}), f32[16,8,512]{2,1,0:T(8,128)}) %reduce-scatter.2.cloned.1.call-update) | async-done | bytes 262160 | tf_op jit(solution)/shard_map/reduce_scatter | solution.py:66
  163.8 1.8 %reshape.44 = f32[16,8,2,256]{3,2,1,0:T(2,128)} reshape(f32[16,8,512]{2,1,0:T(8,128)} %reduce-scatter.2.cloned.1.call-done) | data formatting | bytes 524288 | tf_op jit(solution)/shard_map/reshape | solution.py:67
  (46 shorter events, 8.5 us)
Async XLA Ops:
  7.4 3.2 %copy-start.3 = (bf16[8,2,256,256]{3,2,1,0:T(8,128)(2,1)S(1)}, bf16[8,2,256,256]{3,2,1,0:T(8,128)(2,1)}, u32[]{:S(2)}) copy-start(bf16[8,2,256,256]{3,2,1,0:T(8,128)(2,1)} %param.9) | copy-start | bytes 6291460
  7.4 4.3 %copy-start.7 = (s32[256]{0:T(256)S(1)}, s32[256]{0:T(256)}, u32[]{:S(2)}) copy-start(s32[256]{0:T(256)} %param.11) | copy-start | bytes 3076
  10.6 2.0 %copy-start.6 = (bf16[8,2,256,256]{3,2,1,0:T(8,128)(2,1)S(1)}, bf16[8,2,256,256]{3,2,1,0:T(8,128)(2,1)}, u32[]{:S(2)}) copy-start(bf16[8,2,256,256]{3,2,1,0:T(8,128)(2,1)} %param.8) | copy-start | bytes 6291460
  33.3 7.7 %copy-start.4 = (bf16[8,256,256]{2,1,0:T(8,128)(2,1)S(1)}, bf16[8,256,256]{2,1,0:T(8,128)(2,1)}, u32[]{:S(2)}) copy-start(bf16[8,256,256]{2,1,0:T(8,128)(2,1)} %fusion.6) | copy-start | bytes 3145732
  33.3 7.7 %copy-start.5 = (bf16[8,256,256]{2,1,0:T(8,128)(2,1)S(1)}, bf16[8,256,256]{2,1,0:T(8,128)(2,1)}, u32[]{:S(2)}) copy-start(bf16[8,256,256]{2,1,0:T(8,128)(2,1)} %get-tuple-element.168) | copy-start | bytes 3145732
  42.9 2.4 %copy-start.1 = (bf16[1,256,2,256]{3,2,1,0:T(2,128)(2,1)S(1)}, bf16[1,256,2,256]{3,2,1,0:T(2,128)(2,1)}, u32[]{:S(2)}) copy-start(bf16[1,256,2,256]{3,2,1,0:T(2,128)(2,1)} %param.7) | copy-start | bytes 786436
  42.9 2.4 %copy-start.8 = (s32[1,2,2]{2,1,0:T(2,128)S(1)}, s32[1,2,2]{2,1,0:T(2,128)}, u32[]{:S(2)}) copy-start(s32[1,2,2]{2,1,0:T(2,128)} %param.10) | copy-start | bytes 52
  45.3 29.1 %all-reduce.2.cloned.1.call-start = ((), (), s32[]{:S(2)}) async-start(), calls=%async_computation.3 | async-start | bytes 524288 | tf_op jit(solution)/shard_map/while/body/eval_jaxpr/psum | solution.py:9
  79.8 15.7 %all-to-all-start = ((bf16[16,2,4096]{2,1,0:T(2,128)(2,1)}), bf16[16,2,4096]{2,1,0:T(2,128)(2,1)S(1)}, u32[]{:S(2)}, u32[]{:S(2)}) async-start(bf16[16,2,4096]{2,1,0:T(2,128)(2,1)} %reshape.66), calls=%async_computation | async-start | bytes 524288 | tf_op jit(solution)/shard_map/while/body/eval_jaxpr/all_to_all | solution.py:59
  99.0 1.0 copy-start.2
  99.9 23.8 %all-reduce.2.cloned.1.call-start = ((), (), s32[]{:S(2)}) async-start(), calls=%async_computation.3 | async-start | bytes 524288 | tf_op jit(solution)/shard_map/while/body/eval_jaxpr/psum | solution.py:9
  129.2 15.7 %all-to-all-start = ((bf16[16,2,4096]{2,1,0:T(2,128)(2,1)}), bf16[16,2,4096]{2,1,0:T(2,128)(2,1)S(1)}, u32[]{:S(2)}, u32[]{:S(2)}) async-start(bf16[16,2,4096]{2,1,0:T(2,128)(2,1)} %reshape.66), calls=%async_computation | async-start | bytes 524288 | tf_op jit(solution)/shard_map/while/body/eval_jaxpr/all_to_all | solution.py:59
  148.3 1.0 copy-start.2
  149.3 0.8 copy-start
  149.3 14.5 %reduce-scatter.2.cloned.1.call-start = ((), (), s32[]{:S(2)}) async-start(), calls=%async_computation.2 | async-start | bytes 786432 | tf_op jit(solution)/shard_map/reduce_scatter | solution.py:66
Sparse Core Ops, SparseCore 0:
  48.5 25.8 all-reduce.1
  103.1 20.5 all-reduce.1
Sparse Core Ops, SparseCore 1:
  152.0 11.8 reduce-scatter.1
where the time goes:
time: 174 us; the launch traced here: 173 us
  waiting for transfers between devices  73.3 us (42%)
  local copies, waits for them, and re-layouts  37 us (21%)
  other arithmetic  24.2 us (14%)
  between operations  14.9 us (9%)
  starting transfers between devices  11.3 us (6%)
  loops' own time  8.19 us (5%)
  matrix products  4.28 us (2%)
    psum x2, waiting for transfers between devices, broadcast(): return lax.psum(block, axis)  45.7 us
    all_to_all x2, waiting for transfers between devices, one_block(): lax.all_to_all(product[None, None], 'mode', split_axis=2, concat_axis=1,...  13.8 us
    reduce_scatter x1, waiting for transfers between devices, on_device(): lax.psum_scatter(amplitude, 'cuts', scatter_dimension=1, tiled=True)  13.7 us
    concatenate x1, other arithmetic, widen_first(): return jnp.concatenate([upper, lower], axis=0)  13 us
    unnamed x18, local copies, waits for them, and re-layouts  12.5 us
    all_to_all x2, starting transfers between devices, one_block(): lax.all_to_all(product[None, None], 'mode', split_axis=2, concat_axis=1,...  11.2 us
    another operation x1, loops' own time, on_device(): amplitude = lax.fori_loop(0, block_count, one_block, begin)  8.19 us
    while x12, local copies, waits for them, and re-layouts  5.23 us
  transfers between devices with their start and end apart: 5, of which 5 were waited for; matrix products, arithmetic and copies ran while one was open for 2% of the time, Pallas kernels for 0%

commit v1 on v0

--- a/solution.py
+++ b/solution.py
@@ -56,8 +56,14 @@
             weight_one,
             preferred_element_type=jnp.float32,
         ).astype(jnp.bfloat16)
-        exchanged = lax.all_to_all(
-            product[None, None], "mode", split_axis=2, concat_axis=1, tiled=True
+        exchanged = jnp.concatenate(
+            lax.all_to_all(
+                jnp.stack(jnp.split(product[None, None], lax.axis_size("mode"), axis=2)),
+                "mode",
+                0,
+                0,
+            ),
+            axis=1,
         )
         weight_two = lax.dynamic_index_in_dim(second_all, slice_pair[1], 0, keepdims=True)
         return running + second_step(exchanged, weight_two, contract_cols, free_cols)

time: 174 us -> 182 us (1.046)
  local copies, waits for them, and re-layouts: 37 us -> 49.3 us
  other arithmetic: 24.2 us -> 19.8 us
    while x12 -> x36, local copies, waits for them, and re-layouts: 5.23 us -> 20.1 us
    while x2 -> x0, other arithmetic: 4.41 us -> none
    all_to_all x2 -> x0, local copies, waits for them, and re-layouts: 2.98 us -> none  [one_block(): lax.all_to_all(product[None, None], 'mode', split_axis=2, concat_axis=1,...]
    another operation x2 -> x4, local copies, waits for them, and re-layouts: 3.38 us -> 4.56 us
where the time goes in v1:
time: 182 us; the launch traced here: 181 us
  waiting for transfers between devices  74.1 us (41%)
  local copies, waits for them, and re-layouts  49.3 us (27%)
  other arithmetic  19.8 us (11%)
  between operations  14.9 us (8%)
  starting transfers between devices  11.2 us (6%)
  loops' own time  7.34 us (4%)
  matrix products  4.28 us (2%)
    psum x2, waiting for transfers between devices, broadcast(): return lax.psum(block, axis)  46.2 us
    while x36, local copies, waits for them, and re-layouts  20.1 us
    all_to_all x2, waiting for transfers between devices, one_block(): lax.all_to_all(jnp.stack(jnp.split(product[None, None], lax.axis_size('mo...  14.2 us
    reduce_scatter x1, waiting for transfers between devices, on_device(): lax.psum_scatter(amplitude, 'cuts', scatter_dimension=1, tiled=True)  13.7 us
    concatenate x1, other arithmetic, widen_first(): return jnp.concatenate([upper, lower], axis=0)  13.1 us
    unnamed x18, local copies, waits for them, and re-layouts  12.6 us
    all_to_all x2, starting transfers between devices, one_block(): lax.all_to_all(jnp.stack(jnp.split(product[None, None], lax.axis_size('mo...  11.2 us
    another operation x1, loops' own time, on_device(): amplitude = lax.fori_loop(0, block_count, one_block, begin)  7.34 us
  transfers between devices with their start and end apart: 5, of which 5 were waited for; matrix products, arithmetic and copies ran while one was open for 2% of the time, Pallas kernels for 0%

profile of v1, /device:TPU:0, one launch (start us, length us, event | category | flops | bytes accessed | tf_op | source)
XLA Modules:
  0.0 181.0 jit_solution(142036293469523483)
XLA Ops:
  7.4 3.2 %slice_bitcast_fusion.18 = (bf16[8,256,256]{2,1,0:T(8,128)(2,1)}, bf16[8,256,256]{2,1,0:T(8,128)(2,1)}) fusion(bf16[8,2,256,256]{3,2,1,0:T(8,128)(2,1)} %param.9), kind=kLoop, calls=%fused_computation.51 | loop fusion | bytes 4194304 | tf_op jit(solution)/shard_map/vmap()/squeeze | solution.py:20
  10.6 1.0 fusion.6
  11.7 0.9 copy-done.6
  12.6 3.1 %copy.12 = bf16[8,2,256,256]{2,0,3,1:T(8,128)(2,1)} copy(bf16[8,2,256,256]{3,2,1,0:T(8,128)(2,1)S(1)} %copy-done.6) | data formatting | bytes 4194304 | tf_op args[1]
  15.7 2.4 %gather_fusion = bf16[256,8,2,256]{3,1,2,0:T(8,128)(2,1)S(1)} fusion(bf16[8,2,256,256]{2,0,3,1:T(8,128)(2,1)} %copy.12, s32[1024]{0:T(1024)S(1)} %pad_clamp_fusion), kind=kCustom, calls=%fused_computation | custom fusion | bytes 4195328 | tf_op jit(solution)/shard_map/jit(_take)/gather | solution.py:45
  18.1 0.9 select_bitcast_fusion
  19.1 1.1 slice_bitcast_fusion.16
  20.2 13.1 %maximum_maximum_fusion = bf16[8,512,512]{1,0,2:T(8,128)(2,1)} fusion(bf16[8,256,256]{1,0,2:T(8,128)(2,1)} %get-tuple-element.159, bf16[8,256,256]{1,0,2:T(8,128)(2,1)S(1)} %fusion.7, bf16[8,256,256]{1,0,2:T(8,128)(2,1)S(1)} %get-tuple-element.158), kind=kLoop, calls=%fused_computation.44 | loop fusion | flops 16777216 | bytes 7340032 | tf_op jit(solution)/shard_map/vmap()/concatenate | solution.py:16
  33.3 7.8 %copy.17 = bf16[8,512,512]{2,1,0:T(8,128)(2,1)} copy(bf16[8,512,512]{1,0,2:T(8,128)(2,1)} %maximum_maximum_fusion) | data formatting | bytes 8388608
  41.1 1.9 %maximum_bitcast_fusion.1 = (bf16[1,8,256,512]{3,2,0,1:T(8,128)(2,1)S(1)}, bf16[1,8,256,512]{3,2,0,1:T(8,128)(2,1)S(1)}) fusion(bf16[8,256,256]{2,1,0:T(8,128)(2,1)S(1)} %copy-done.5, bf16[8,256,256]{2,1,0:T(8,128)(2,1)} %get-tuple-element.157, bf16[8,256,256]{2,1,0:T(8,128)(2,1)S(1)} %copy-done.4), kind=kLoop, calls=%fused_computation.46 | loop fusion | flops 8388608 | bytes 7340032 | tf_op jit(solution)/shard_map/vmap()/stack | solution.py:23
  43.0 2.3 %maximum_bitcast_fusion = bf16[8,2,256,512]{3,2,1,0:T(8,128)(2,1)} fusion(bf16[1,8,256,512]{3,2,0,1:T(8,128)(2,1)S(1)} %get-tuple-element.161, bf16[1,8,256,512]{3,2,0,1:T(8,128)(2,1)S(1)} %get-tuple-element.160), kind=kLoop, calls=%fused_computation.45 | loop fusion | flops 2097152 | bytes 8388608 | tf_op jit(solution)/shard_map/vmap()/transpose | solution.py:46
  45.4 111.8 %while.14 = (s32[]{:T(128)}, f32[16,16,512]{2,1,0:T(8,128)S(1)}, bf16[1,256,2,256]{3,2,1,0:T(2,128)(2,1)S(1)}, s32[2,2]{1,0:T(2,128)S(1)}, bf16[8,512,512]{2,1,0...) while((s32[]{:T(128)}, f32[16,16,512]{2,1,0:T(8,128)S(1)}, ...), condition=%wide.region_2.3_spmd.clone, body=%wide.region_0.0_spmd.clone.sunk | while | flops 269090816 | bytes 9437565 | solution.py:71
  45.6 0.7 copy.32
  46.4 0.6 fusion.22
  48.7 25.8 %all-reduce.2.cloned.1.call-done = bf16[256,512]{1,0:T(8,128)(2,1)} async-done(((bf16[256,512]{1,0:T(8,128)(2,1)}), bf16[256,512]{1,0:T(8,128)(2,1)}) %all-reduce.2.cloned.1.call-update) | async-done | bytes 262160 | tf_op jit(solution)/shard_map/while/body/eval_jaxpr/psum | solution.py:9
  74.5 1.4 fusion.23
  85.6 5.6 %all-to-all-start = ((bf16[16,1,1,16,512]{4,3,2,1,0:T(8,128)(2,1)}), bf16[16,1,1,16,512]{4,3,2,1,0:T(8,128)(2,1)S(1)}, u32[]{:S(2)}, u32[]{:S(2)}) async-start(bf16[16,1,1,16,512]{4,3,2,1,0:T(8,128)(2,1)} %constant_dynamic-update-slice_fusion.47), calls=%async_computation | async-start | bytes 524288 | tf_op jit(solution)/shard_map/while/body/eval_jaxpr/all_to_all | solution.py:60
  93.1 1.1 constant_dynamic-slice_fusion.5
  94.2 7.1 %all-to-all-done = bf16[16,1,1,16,512]{4,3,2,1,0:T(8,128)(2,1)S(1)} async-done(((bf16[16,1,1,16,512]{4,3,2,1,0:T(8,128)(2,1)}), bf16[16,1,1,16,512]{4,3,2,1,0:T(8,128)(2,1)S(1)}, u32[]{:S(2)}, u32[]{:S(2)}) %all-to-all-start) | async-done | bytes 262176 | tf_op jit(solution)/shard_map/while/body/eval_jaxpr/all_to_all | solution.py:60
  101.3 1.7 reshape.57
  103.0 0.7 fusion.24
  104.1 0.7 copy.32
  107.3 20.4 %all-reduce.2.cloned.1.call-done = bf16[256,512]{1,0:T(8,128)(2,1)} async-done(((bf16[256,512]{1,0:T(8,128)(2,1)}), bf16[256,512]{1,0:T(8,128)(2,1)}) %all-reduce.2.cloned.1.call-update) | async-done | bytes 262160 | tf_op jit(solution)/shard_map/while/body/eval_jaxpr/psum | solution.py:9
  127.7 1.4 fusion.23
  138.9 5.6 %all-to-all-start = ((bf16[16,1,1,16,512]{4,3,2,1,0:T(8,128)(2,1)}), bf16[16,1,1,16,512]{4,3,2,1,0:T(8,128)(2,1)S(1)}, u32[]{:S(2)}, u32[]{:S(2)}) async-start(bf16[16,1,1,16,512]{4,3,2,1,0:T(8,128)(2,1)} %constant_dynamic-update-slice_fusion.47), calls=%async_computation | async-start | bytes 524288 | tf_op jit(solution)/shard_map/while/body/eval_jaxpr/all_to_all | solution.py:60
  146.4 1.1 constant_dynamic-slice_fusion.5
  147.5 7.1 %all-to-all-done = bf16[16,1,1,16,512]{4,3,2,1,0:T(8,128)(2,1)S(1)} async-done(((bf16[16,1,1,16,512]{4,3,2,1,0:T(8,128)(2,1)}), bf16[16,1,1,16,512]{4,3,2,1,0:T(8,128)(2,1)S(1)}, u32[]{:S(2)}, u32[]{:S(2)}) %all-to-all-start) | async-done | bytes 262176 | tf_op jit(solution)/shard_map/while/body/eval_jaxpr/all_to_all | solution.py:60
  154.5 1.7 reshape.57
  156.2 0.7 fusion.24
  157.2 0.8 copy-done
  158.0 13.7 %reduce-scatter.2.cloned.1.call-done = f32[16,8,512]{2,1,0:T(8,128)} async-done(((f32[16,16,512]{2,1,0:T(8,128)}), f32[16,8,512]{2,1,0:T(8,128)}) %reduce-scatter.2.cloned.1.call-update) | async-done | bytes 262160 | tf_op jit(solution)/shard_map/reduce_scatter | solution.py:72
  171.7 1.8 %reshape.40 = f32[16,8,2,256]{3,2,1,0:T(2,128)} reshape(f32[16,8,512]{2,1,0:T(8,128)} %reduce-scatter.2.cloned.1.call-done) | data formatting | bytes 524288 | tf_op jit(solution)/shard_map/reshape | solution.py:73
  (66 shorter events, 21.1 us)
Async XLA Ops:
  7.4 3.3 %copy-start.3 = (bf16[8,2,256,256]{3,2,1,0:T(8,128)(2,1)S(1)}, bf16[8,2,256,256]{3,2,1,0:T(8,128)(2,1)}, u32[]{:S(2)}) copy-start(bf16[8,2,256,256]{3,2,1,0:T(8,128)(2,1)} %param.9) | copy-start | bytes 6291460
  7.4 4.3 %copy-start.7 = (s32[256]{0:T(256)S(1)}, s32[256]{0:T(256)}, u32[]{:S(2)}) copy-start(s32[256]{0:T(256)} %param.11) | copy-start | bytes 3076
  10.6 2.0 %copy-start.6 = (bf16[8,2,256,256]{3,2,1,0:T(8,128)(2,1)S(1)}, bf16[8,2,256,256]{3,2,1,0:T(8,128)(2,1)}, u32[]{:S(2)}) copy-start(bf16[8,2,256,256]{3,2,1,0:T(8,128)(2,1)} %param.8) | copy-start | bytes 6291460
  33.3 7.8 %copy-start.4 = (bf16[8,256,256]{2,1,0:T(8,128)(2,1)S(1)}, bf16[8,256,256]{2,1,0:T(8,128)(2,1)}, u32[]{:S(2)}) copy-start(bf16[8,256,256]{2,1,0:T(8,128)(2,1)} %fusion.6) | copy-start | bytes 3145732
  33.3 7.8 %copy-start.5 = (bf16[8,256,256]{2,1,0:T(8,128)(2,1)S(1)}, bf16[8,256,256]{2,1,0:T(8,128)(2,1)}, u32[]{:S(2)}) copy-start(bf16[8,256,256]{2,1,0:T(8,128)(2,1)} %get-tuple-element.156) | copy-start | bytes 3145732
  43.0 2.4 %copy-start.1 = (bf16[1,256,2,256]{3,2,1,0:T(2,128)(2,1)S(1)}, bf16[1,256,2,256]{3,2,1,0:T(2,128)(2,1)}, u32[]{:S(2)}) copy-start(bf16[1,256,2,256]{3,2,1,0:T(2,128)(2,1)} %param.7) | copy-start | bytes 786436
  43.0 2.4 %copy-start.8 = (s32[1,2,2]{2,1,0:T(2,128)S(1)}, s32[1,2,2]{2,1,0:T(2,128)}, u32[]{:S(2)}) copy-start(s32[1,2,2]{2,1,0:T(2,128)} %param.10) | copy-start | bytes 52
  45.4 29.1 %all-reduce.2.cloned.1.call-start = ((), (), s32[]{:S(2)}) async-start(), calls=%async_computation.3 | async-start | bytes 524288 | tf_op jit(solution)/shard_map/while/body/eval_jaxpr/psum | solution.py:9
  85.6 15.7 %all-to-all-start = ((bf16[16,1,1,16,512]{4,3,2,1,0:T(8,128)(2,1)}), bf16[16,1,1,16,512]{4,3,2,1,0:T(8,128)(2,1)S(1)}, u32[]{:S(2)}, u32[]{:S(2)}) async-start(bf16[16,1,1,16,512]{4,3,2,1,0:T(8,128)(2,1)} %constant_dynamic-update-slice_fusion.47), calls=%async_computation | async-start | bytes 524288 | tf_op jit(solution)/shard_map/while/body/eval_jaxpr/all_to_all | solution.py:60
  103.0 1.0 copy-start.2
  103.9 23.8 %all-reduce.2.cloned.1.call-start = ((), (), s32[]{:S(2)}) async-start(), calls=%async_computation.3 | async-start | bytes 524288 | tf_op jit(solution)/shard_map/while/body/eval_jaxpr/psum | solution.py:9
  138.9 15.7 %all-to-all-start = ((bf16[16,1,1,16,512]{4,3,2,1,0:T(8,128)(2,1)}), bf16[16,1,1,16,512]{4,3,2,1,0:T(8,128)(2,1)S(1)}, u32[]{:S(2)}, u32[]{:S(2)}) async-start(bf16[16,1,1,16,512]{4,3,2,1,0:T(8,128)(2,1)} %constant_dynamic-update-slice_fusion.47), calls=%async_computation | async-start | bytes 524288 | tf_op jit(solution)/shard_map/while/body/eval_jaxpr/all_to_all | solution.py:60
  156.2 1.0 copy-start.2
  157.2 0.8 copy-start
  157.2 14.5 %reduce-scatter.2.cloned.1.call-start = ((), (), s32[]{:S(2)}) async-start(), calls=%async_computation.2 | async-start | bytes 786432 | tf_op jit(solution)/shard_map/reduce_scatter | solution.py:72
Sparse Core Ops, SparseCore 0:
  48.6 25.8 all-reduce.1
  107.1 20.5 all-reduce.1
Sparse Core Ops, SparseCore 1:
  159.9 11.8 reduce-scatter.1
